TPU v7x, 256 devices: a whole 4x4x8 slice. The times are simulated.
256 devices in a mesh: rows: 16 (over x, y), sub: 16 (over z, core).
Axes of the slice: x: 4, y: 4, z: 8, core: 2. Of those that a mesh axis runs over, the one named last changes fastest.
Arguments:
- embeddings: bfloat16 [65536, 1024], P(('rows', 'sub'))
- codes: int32 [64, 65536], P(None, ('rows', 'sub')), may hold values from 0 to 255
- codebook: bfloat16 [256, 1024], P(None, 'sub'), may hold values from -6 to 6
Outputs:
- rotation: float32 [1024, 1024], P('sub')
- rotated: bfloat16 [65536, 1024], P(('rows', 'sub'))
- new_codebook: float32 [256, 1024], P(None, 'sub')
All inputs are finite; a program needn't handle non-finite values.
Results may differ from a plain program's by a relative error of at most 0.0095.
Values may be sent and summed in bfloat16 or wider, within the bound.
No kernel may reach another device: no remote copies, remote signals or barrier semaphores. Data moves between devices by JAX's collectives and lax.ppermute only.
A program may use at most 64 MiB of HBM per device.

v0:
```python
import math
import jax
import jax.numpy as jnp
from jax import lax
from jax.sharding import PartitionSpec as P

NS_STEPS = 3
coef_a = 3.4445
coef_b = -4.775
coef_c = 2.0315
frob_eps = 1e-07
highest = lax.Precision.HIGHEST


def rows_dot(left, right):
    return lax.dot_general(
        left, right, (((1,), (1,)), ((), ())), precision=highest, preferred_element_type=jnp.float32
    )


def one_hot_codes(code_block, count_codes):
    levels = lax.broadcasted_iota(jnp.int32, code_block.shape + (count_codes,), 2)
    return (code_block[:, :, None] == levels).astype(jnp.bfloat16)


def decode_rows(codes, table):
    subspaces, local_rows = codes.shape
    count_codes, row_width = table.shape
    sub_width = row_width // subspaces
    block_rows = math.gcd(local_rows, 32768 // subspaces)
    blocks = local_rows // block_rows
    codewords = table.reshape(count_codes, subspaces, sub_width)
    code_blocks = codes.reshape(subspaces, blocks, block_rows).transpose(1, 0, 2)

    def decode_block(unused, code_block):
        one_hot = one_hot_codes(code_block, count_codes)
        picked = jnp.einsum("mnk,kmj->nmj", one_hot, codewords, preferred_element_type=jnp.float32)
        return (unused, picked.reshape(block_rows, row_width).astype(jnp.bfloat16))

    unused, decoded = lax.scan(decode_block, jnp.zeros((), jnp.float32), code_blocks)
    return decoded.reshape(local_rows, row_width)


def codeword_totals(codes, row_values, count_codes):
    subspaces, total_rows = codes.shape
    row_width = row_values.shape[1]
    sub_width = row_width // subspaces
    block_rows = math.gcd(total_rows, 32768 // subspaces)
    blocks = total_rows // block_rows
    code_blocks = codes.reshape(subspaces, blocks, block_rows).transpose(1, 0, 2)
    row_blocks = row_values.reshape(blocks, block_rows, subspaces, sub_width)

    def accumulate(running, pieces):
        one_hot = one_hot_codes(pieces[0], count_codes)
        block_sums = jnp.einsum(
            "mnk,nmj->kmj", one_hot, pieces[1], preferred_element_type=jnp.float32
        )
        block_counts = jnp.sum(one_hot, axis=1, dtype=jnp.float32).T
        return ((running[0] + block_sums, running[1] + block_counts), None)

    initial = (
        jnp.zeros((count_codes, subspaces, sub_width), jnp.float32),
        jnp.zeros((count_codes, subspaces), jnp.float32),
    )
    (code_sums, counts), unused = lax.scan(accumulate, initial, (code_blocks, row_blocks))
    return (code_sums.reshape(count_codes, row_width), counts)


def newton_panel(panel, whole):
    gram_rows = rows_dot(panel, whole)
    quartic = rows_dot(
        jnp.dot(gram_rows, whole, precision=highest, preferred_element_type=jnp.float32), whole
    )
    mixer = coef_b * gram_rows + coef_c * quartic
    return coef_a * panel + jnp.dot(
        mixer, whole, precision=highest, preferred_element_type=jnp.float32
    )


def collect(panel):
    return lax.all_gather(panel, "sub", axis=0, tiled=True)


def body(embeddings, codes, codebook):
    table = lax.all_gather(codebook, "sub", axis=1, tiled=True)
    decoded = decode_rows(codes, table)
    partial_panel = lax.psum_scatter(
        lax.dot_general(
            embeddings, decoded, (((0,), (0,)), ((), ())), preferred_element_type=jnp.float32
        ),
        "sub",
        scatter_dimension=0,
        tiled=True,
    )
    cross_panel = lax.psum(partial_panel, "rows")
    squares = lax.psum(jnp.sum(cross_panel * cross_panel), "sub")
    frob_scale = jnp.sqrt(squares) + frob_eps
    panel = cross_panel / frob_scale
    whole = collect(panel)
    for newton_step in range(NS_STEPS):
        if newton_step > 0:
            whole = collect(panel)
        panel = newton_panel(panel, whole)
    rotation_full = lax.all_gather(panel.astype(jnp.bfloat16), "sub", axis=0, tiled=True)
    rotated = jnp.dot(embeddings, rotation_full, preferred_element_type=jnp.float32).astype(
        jnp.bfloat16
    )
    moved_rows = lax.all_to_all(rotated, "sub", split_axis=1, concat_axis=0, tiled=True)
    moved_codes = lax.all_to_all(codes, "sub", split_axis=0, concat_axis=1, tiled=True)
    code_sums, counts = codeword_totals(moved_codes, moved_rows, table.shape[0])
    code_sums, counts = (
        lax.psum(code_sums.astype(jnp.bfloat16), "rows").astype(jnp.float32),
        lax.psum(counts.astype(jnp.bfloat16), "rows").astype(jnp.float32),
    )
    own_codebook = codebook.astype(jnp.float32)
    spread = jnp.repeat(counts, own_codebook.shape[1] // counts.shape[1], axis=1)
    new_codebook = (code_sums + own_codebook) / (spread + 1.0)
    return (panel, rotated, new_codebook)


def solution(mesh):
    in_specs = (P(("rows", "sub"), None), P(None, ("rows", "sub")), P(None, "sub"))
    out_specs = (P("sub", None), P(("rows", "sub"), None), P(None, "sub"))
    return jax.shard_map(body, mesh=mesh, in_specs=in_specs, out_specs=out_specs, check_vma=False)
```

profile of v0, /device:TPU:64, one launch (start us, length us, event | category | flops | bytes accessed | tf_op | source)
XLA Modules:
  0.0 547.7 jit_solution(3402713358330620616)
XLA Ops:
  7.2 18.8 %all_gather.15 = bf16[256,1024]{0,1:T(8,128)(2,1)S(1)} all-gather(bf16[256,64]{0,1:T(8,128)(2,1)} %param.5), channel_id=1, replica_groups=mesh['rows'=16,'sub'=16] {'sub'}, dimensions={1}, use_global_device_ids=true | all-gather | bytes 557056 | tf_op jit(solution)/shard_map/all_gather | solution.py:85
  26.0 5.3 fusion.6
  34.0 5.4 copy.15
  39.4 58.3 %reduce-scatter.4.cloned.1.call-done = f32[64,1024]{1,0:T(8,128)} async-done(((f32[1024,1024]{1,0:T(8,128)}), f32[64,1024]{1,0:T(8,128)}) %reduce-scatter.4.cloned.1.call-update) | async-done | bytes 262160 | tf_op jit(solution)/shard_map/reduce_scatter | solution.py:87
  97.8 102.1 %all-reduce.3.cloned.1.call-done = f32[64,1024]{1,0:T(8,128)} async-done(((f32[64,1024]{1,0:T(8,128)}), f32[64,1024]{1,0:T(8,128)}) %all-reduce.3.cloned.1.call-update) | async-done | bytes 262160 | tf_op jit(solution)/shard_map/psum | solution.py:95
  201.5 21.1 %psum.29 = f32[]{:T(128)} all-reduce(f32[]{:T(128)} %multiply_reduce_fusion), channel_id=1, replica_groups=mesh['rows'=16,'sub'=16] {'sub'}, use_global_device_ids=true, to_apply=%region_3.4 | all-reduce | flops 1 | bytes 8 | tf_op jit(solution)/shard_map/psum | solution.py:96
  225.0 43.2 %all-gather.5.cloned.1.call-done = f32[1024,1024]{1,0:T(8,128)} async-done(((f32[64,1024]{1,0:T(8,128)}), f32[1024,1024]{1,0:T(8,128)}) %all-gather.5.cloned.1.call-update) | async-done | bytes 4194320 | tf_op jit(solution)/shard_map/all_gather | solution.py:81
  268.2 6.5 %fusion.12 = f32[64,1024]{1,0:T(8,128)S(1)} fusion(f32[64,1024]{1,0:T(8,128)} %broadcast_divide_fusion, f32[1024,1024]{1,0:T(8,128)} %all-gather.5.cloned.1.call-done), kind=kOutput, calls=%fused_computation.26 | convolution fusion | flops 805306368 | bytes 4718592 | tf_op jit(solution)/shard_map/dot_general | solution.py:16
  277.4 4.2 fusion.9
  281.6 3.4 convolution_add_fusion.2
  285.5 40.1 %all-gather.7.cloned.1.call-done = f32[1024,1024]{1,0:T(8,128)} async-done(((f32[64,1024]{1,0:T(8,128)}), f32[1024,1024]{1,0:T(8,128)}) %all-gather.7.cloned.1.call-update) | async-done | bytes 4194320 | tf_op jit(solution)/shard_map/all_gather | solution.py:81
  325.5 6.5 %fusion.14 = f32[64,1024]{1,0:T(8,128)S(1)} fusion(f32[64,1024]{1,0:T(8,128)} %convolution_add_fusion.2, f32[1024,1024]{1,0:T(8,128)} %all-gather.7.cloned.1.call-done), kind=kOutput, calls=%fused_computation.28 | convolution fusion | flops 805306368 | bytes 4718592 | tf_op jit(solution)/shard_map/dot_general | solution.py:16
  334.7 4.2 fusion.8
  338.9 3.4 convolution_add_fusion.1
  342.5 40.4 %all-gather.9.cloned.1.call-done = f32[1024,1024]{1,0:T(8,128)} async-done(((f32[64,1024]{1,0:T(8,128)}), f32[1024,1024]{1,0:T(8,128)}) %all-gather.9.cloned.1.call-update) | async-done | bytes 4194320 | tf_op jit(solution)/shard_map/all_gather | solution.py:81
  382.8 6.5 %fusion.16 = f32[64,1024]{1,0:T(8,128)S(1)} fusion(f32[64,1024]{1,0:T(8,128)} %convolution_add_fusion.1, f32[1024,1024]{1,0:T(8,128)} %all-gather.9.cloned.1.call-done), kind=kOutput, calls=%fused_computation.30 | convolution fusion | flops 805306368 | bytes 4718592 | tf_op jit(solution)/shard_map/dot_general | solution.py:16
  392.0 4.2 fusion.7
  396.2 3.4 fusion.11
  400.3 6.0 %all-to-all-start.1 = ((s32[16,4,256]{2,1,0:T(4,128)}), s32[16,4,256]{2,1,0:T(4,128)S(1)}, u32[]{:S(2)}, u32[]{:S(2)}) async-start(s32[16,4,256]{2,1,0:T(4,128)} %all_to_all.27), calls=%async_computation.1 | async-start | bytes 131072 | tf_op jit(solution)/shard_map/all_to_all | solution.py:109
  406.3 31.3 %all-gather.11.cloned.1.call-done = bf16[1024,1024]{1,0:T(8,128)(2,1)} async-done(((bf16[64,1024]{1,0:T(8,128)(2,1)}), bf16[1024,1024]{1,0:T(8,128)(2,1)}) %all-gather.11.cloned.1.call-update) | async-done | bytes 2097168 | tf_op jit(solution)/shard_map/all_gather | solution.py:104
  440.8 6.4 %all-to-all-start = ((bf16[256,16,64]{0,2,1:T(8,128)(2,1)}), bf16[256,16,64]{0,2,1:T(8,128)(2,1)S(1)}, u32[]{:S(2)}, u32[]{:S(2)}) async-start(bf16[256,16,64]{0,2,1:T(8,128)(2,1)} %bitcast.5), calls=%async_computation | async-start | bytes 1048576 | tf_op jit(solution)/shard_map/all_to_all | solution.py:108
  447.1 6.9 %fusion.3 = bf16[4,256]{1,0:T(4,128)(2,1)S(1)} fusion(s32[4,4096]{1,0:T(4,128)S(1)} %bitcast.55), kind=kLoop, calls=%fused_computation.5 | loop fusion | flops 12581888 | bytes 67584 | tf_op jit(solution)/shard_map/while/body/eval_jaxpr/reduce_sum | solution.py:58
  456.1 5.9 %all-to-all-done = bf16[256,16,64]{0,2,1:T(8,128)(2,1)S(1)} async-done(((bf16[256,16,64]{0,2,1:T(8,128)(2,1)}), bf16[256,16,64]{0,2,1:T(8,128)(2,1)S(1)}, u32[]{:S(2)}, u32[]{:S(2)}) %all-to-all-start) | async-done | bytes 524320 | tf_op jit(solution)/shard_map/all_to_all | solution.py:108
  465.8 74.2 %all-reduce = (bf16[256,64]{0,1:T(8,128)(2,1)S(1)}, bf16[256,4]{0,1:T(4,128)(2,1)S(1)}) all-reduce(bf16[256,64]{0,1:T(8,128)(2,1)S(1)} %bitcast.57, bf16[256,4]{0,1:T(4,128)(2,1)S(1)} %bitcast.58), channel_id=1, replica_groups=mesh['rows'=16,'sub'=16] {'rows'}, use_global_device_ids=true, to_apply=%region_4.5 | all-reduce | flops 17408 | bytes 69632 | tf_op jit(solution)/shard_map/psum | solution.py:112
  (45 shorter events, 25.2 us)
Async XLA Ops:
  7.2 24.1 %copy-start = (bf16[256,1024]{1,0:T(8,128)(2,1)S(1)}, bf16[256,1024]{1,0:T(8,128)(2,1)}, u32[]{:S(2)}) copy-start(bf16[256,1024]{1,0:T(8,128)(2,1)} %param.3) | copy-start | bytes 1572868
  7.2 90.5 %reduce-scatter.4.cloned.1.call-start = ((), (), s32[]{:S(2)}) async-start(), calls=%async_computation.8 | async-start | bytes 4456448 | tf_op jit(solution)/shard_map/reduce_scatter | solution.py:87
  39.4 160.5 %all-reduce.3.cloned.1.call-start = ((), (), s32[]{:S(2)}) async-start(), calls=%async_computation.3 | async-start | bytes 524288 | tf_op jit(solution)/shard_map/psum | solution.py:95
  97.7 170.5 %all-gather.5.cloned.1.call-start = ((), (), s32[]{:S(2)}) async-start(), calls=%async_computation.4 | async-start | bytes 4456448 | tf_op jit(solution)/shard_map/all_gather | solution.py:81
  225.0 100.6 %all-gather.7.cloned.1.call-start = ((), (), s32[]{:S(2)}) async-start(), calls=%async_computation.5 | async-start | bytes 4456448 | tf_op jit(solution)/shard_map/all_gather | solution.py:81
  268.2 6.5 %copy-start.2 = (f32[1024,1024]{1,0:T(8,128)S(1)}, f32[1024,1024]{1,0:T(8,128)}, u32[]{:S(2)}) copy-start(f32[1024,1024]{1,0:T(8,128)} %all-gather.5.cloned.1.call-done) | copy-start | bytes 12582916
  274.7 6.8 %copy-start.6 = (f32[64,1024]{1,0:T(8,128)S(1)}, f32[64,1024]{1,0:T(8,128)}, u32[]{:S(2)}) copy-start(f32[64,1024]{1,0:T(8,128)} %broadcast_divide_fusion) | copy-start | bytes 786436
  285.0 97.9 %all-gather.9.cloned.1.call-start = ((), (), s32[]{:S(2)}) async-start(), calls=%async_computation.6 | async-start | bytes 4456448 | tf_op jit(solution)/shard_map/all_gather | solution.py:81
  325.5 6.5 %copy-start.3 = (f32[1024,1024]{1,0:T(8,128)S(1)}, f32[1024,1024]{1,0:T(8,128)}, u32[]{:S(2)}) copy-start(f32[1024,1024]{1,0:T(8,128)} %all-gather.7.cloned.1.call-done) | copy-start | bytes 12582916
  332.0 6.8 %copy-start.5 = (f32[64,1024]{1,0:T(8,128)S(1)}, f32[64,1024]{1,0:T(8,128)}, u32[]{:S(2)}) copy-start(f32[64,1024]{1,0:T(8,128)} %convolution_add_fusion.2) | copy-start | bytes 786436
  342.2 95.4 %all-gather.11.cloned.1.call-start = ((), (), s32[]{:S(2)}) async-start(), calls=%async_computation.7 | async-start | bytes 2228224 | tf_op jit(solution)/shard_map/all_gather | solution.py:104
  382.8 6.5 %copy-start.1 = (f32[1024,1024]{1,0:T(8,128)S(1)}, f32[1024,1024]{1,0:T(8,128)}, u32[]{:S(2)}) copy-start(f32[1024,1024]{1,0:T(8,128)} %all-gather.9.cloned.1.call-done) | copy-start | bytes 12582916
  389.3 6.9 %copy-start.4 = (f32[64,1024]{1,0:T(8,128)S(1)}, f32[64,1024]{1,0:T(8,128)}, u32[]{:S(2)}) copy-start(f32[64,1024]{1,0:T(8,128)} %convolution_add_fusion.1) | copy-start | bytes 786436
  392.0 7.6 %copy-start.8 = (s32[64,256]{1,0:T(8,128)S(1)}, s32[64,256]{1,0:T(8,128)}, u32[]{:S(2)}) copy-start(s32[64,256]{1,0:T(8,128)} %param.4) | copy-start | bytes 196612
  400.3 40.5 %all-to-all-start.1 = ((s32[16,4,256]{2,1,0:T(4,128)}), s32[16,4,256]{2,1,0:T(4,128)S(1)}, u32[]{:S(2)}, u32[]{:S(2)}) async-start(s32[16,4,256]{2,1,0:T(4,128)} %all_to_all.27), calls=%async_computation.1 | async-start | bytes 131072 | tf_op jit(solution)/shard_map/all_to_all | solution.py:109
  440.8 21.2 %all-to-all-start = ((bf16[256,16,64]{0,2,1:T(8,128)(2,1)}), bf16[256,16,64]{0,2,1:T(8,128)(2,1)S(1)}, u32[]{:S(2)}, u32[]{:S(2)}) async-start(bf16[256,16,64]{0,2,1:T(8,128)(2,1)} %bitcast.5), calls=%async_computation | async-start | bytes 1048576 | tf_op jit(solution)/shard_map/all_to_all | solution.py:108
  456.1 83.9 %copy-start.7 = (bf16[256,64]{0,1:T(8,128)(2,1)S(1)}, bf16[256,64]{0,1:T(8,128)(2,1)}, u32[]{:S(2)}) copy-start(bf16[256,64]{0,1:T(8,128)(2,1)} %param.5) | copy-start | bytes 98308
Sparse Core Ops, SparseCore 0:
  39.5 58.1 reduce-scatter.3
  100.9 98.9 all-reduce.2
  225.1 43.1 all-gather.4
  285.1 40.4 all-gather.6
  342.4 40.4 all-gather.8
  399.7 37.8 all-gather.10
where the time goes:
time: 557 us; the launch traced here: 548 us
  waiting for transfers between devices  321 us (58%)
  blocking collectives  114 us (20%)
  matrix products  64.3 us (12%)
  between operations  15.2 us (3%)
  starting transfers between devices  13.3 us (2%)
  other arithmetic  10.9 us (2%)
  local copies, waits for them, and re-layouts  8.64 us (2%)
    all_gather x3, waiting for transfers between devices, collect(): return lax.all_gather(panel, 'sub', axis=0, tiled=True)  124 us
    psum x1, waiting for transfers between devices, body(): cross_panel = lax.psum(partial_panel, 'rows')  102 us
    psum x1, blocking collectives, body(): lax.psum(code_sums.astype(jnp.bfloat16), 'rows').astype(jnp.float32)  74.2 us
    reduce_scatter x1, waiting for transfers between devices, body(): lax.psum_scatter(lax.dot_general(embeddings, decoded, (((0,), (0,)), ((),...  58.3 us
    dot_general x6, matrix products, rows_dot(): lax.dot_general(left, right, (((1,), (1,)), ((), ())), precision=highest,...  31.9 us
    all_gather x1, waiting for transfers between devices, body(): lax.all_gather(panel.astype(jnp.bfloat16), 'sub', axis=0, tiled=True)  31.3 us
    psum x1, blocking collectives, body(): squares = lax.psum(jnp.sum(cross_panel * cross_panel), 'sub')  21.1 us
    all_gather x1, blocking collectives, body(): table = lax.all_gather(codebook, 'sub', axis=1, tiled=True)  18.8 us
  transfers between devices with their start and end apart: 8, of which 7 were waited for; matrix products, arithmetic and copies ran while one was open for 2% of the time, Pallas kernels for 0%

commit v1 on v0

--- a/solution.py
+++ b/solution.py
@@ -92,7 +92,11 @@
         scatter_dimension=0,
         tiled=True,
     )
-    cross_panel = lax.psum(partial_panel, "rows")
+    cross_panel = partial_panel
+    for hop in (1, 2, 4, 8):
+        cross_panel = cross_panel + lax.ppermute(
+            cross_panel, "rows", [(dev, dev ^ hop) for dev in range(16)]
+        )
     squares = lax.psum(jnp.sum(cross_panel * cross_panel), "sub")
     frob_scale = jnp.sqrt(squares) + frob_eps
     panel = cross_panel / frob_scale

time: 557 us -> 487 us (0.87)
  waiting for transfers between devices: 321 us -> 248 us
  starting transfers between devices: 13.3 us -> 22.9 us
    psum x1 -> x0, waiting for transfers between devices: 102 us -> none  [body(): cross_panel = lax.psum(partial_panel, 'rows')]
    ppermute x0 -> x4, waiting for transfers between devices: none -> 26.5 us  [body(): lax.ppermute(cross_panel, 'rows', [(dev, dev ^ hop) for dev in range(16)])]
    ppermute x0 -> x4, starting transfers between devices: none -> 9.39 us  [body(): lax.ppermute(cross_panel, 'rows', [(dev, dev ^ hop) for dev in range(16)])]
  transfers between devices with their start and end apart: 8 -> 11, of which waited for: 7 -> 10; matrix products, arithmetic and copies ran while one was open for 2% -> 3% of each run, Pallas kernels for 0% -> 0%
where the time goes in v1:
time: 487 us; the launch traced here: 482 us
  waiting for transfers between devices  248 us (51%)
  blocking collectives  114 us (23%)
  matrix products  64.3 us (13%)
  starting transfers between devices  22.9 us (5%)
  between operations  14.9 us (3%)
  other arithmetic  10 us (2%)
  local copies, waits for them, and re-layouts  8.64 us (2%)
    all_gather x3, waiting for transfers between devices, collect(): return lax.all_gather(panel, 'sub', axis=0, tiled=True)  126 us
    psum x1, blocking collectives, body(): lax.psum(code_sums.astype(jnp.bfloat16), 'rows').astype(jnp.float32)  74.2 us
    reduce_scatter x1, waiting for transfers between devices, body(): lax.psum_scatter(lax.dot_general(embeddings, decoded, (((0,), (0,)), ((),...  58.1 us
    dot_general x6, matrix products, rows_dot(): lax.dot_general(left, right, (((1,), (1,)), ((), ())), precision=highest,...  31.9 us
    all_gather x1, waiting for transfers between devices, body(): lax.all_gather(panel.astype(jnp.bfloat16), 'sub', axis=0, tiled=True)  31.3 us
    ppermute x4, waiting for transfers between devices, body(): lax.ppermute(cross_panel, 'rows', [(dev, dev ^ hop) for dev in range(16)])  26.5 us
    psum x1, blocking collectives, body(): squares = lax.psum(jnp.sum(cross_panel * cross_panel), 'sub')  20.7 us
    all_gather x1, blocking collectives, body(): table = lax.all_gather(codebook, 'sub', axis=1, tiled=True)  18.8 us
  transfers between devices with their start and end apart: 11, of which 10 were waited for; matrix products, arithmetic and copies ran while one was open for 3% of the time, Pallas kernels for 0%

profile of v1, /device:TPU:64, one launch (start us, length us, event | category | flops | bytes accessed | tf_op | source)
XLA Modules:
  0.0 482.5 jit_solution(1768068852819949441)
XLA Ops:
  7.2 18.8 %all_gather.15 = bf16[256,1024]{0,1:T(8,128)(2,1)S(1)} all-gather(bf16[256,64]{0,1:T(8,128)(2,1)} %param.5), channel_id=1, replica_groups=mesh['rows'=16,'sub'=16] {'sub'}, dimensions={1}, use_global_device_ids=true | all-gather | bytes 557056 | tf_op jit(solution)/shard_map/all_gather | solution.py:85
  26.0 5.3 %fusion.6 = bf16[64,256,16]{1,2,0:T(8,128)(2,1)S(1)} fusion(bf16[256,64,16]{0,2,1:T(8,128)(2,1)S(1)} %bitcast.53, s32[64,256]{1,0:T(8,128)} %param.4), kind=kOutput, calls=%fused_computation.9 | convolution fusion | flops 138674176 | bytes 1114112 | tf_op jit(solution)/shard_map/while/body/eval_jaxpr/mnk,kmj->nmj/dot_general | solution.py:37
  34.0 5.4 %copy.16 = f32[1024,1024]{1,0:T(8,128)} copy(f32[1024,1024]{0,1:T(8,128)} %convolution_bitcast_fusion) | data formatting | bytes 8388608
  39.4 58.1 %reduce-scatter.4.cloned.1.call-done = f32[64,1024]{1,0:T(8,128)} async-done(((f32[1024,1024]{1,0:T(8,128)}), f32[64,1024]{1,0:T(8,128)}) %reduce-scatter.4.cloned.1.call-update) | async-done | bytes 262160 | tf_op jit(solution)/shard_map/reduce_scatter | solution.py:87
  99.0 5.6 %collective-permute-done = f32[64,1024]{1,0:T(8,128)S(1)} collective-permute-done((f32[64,1024]{1,0:T(8,128)}, f32[64,1024]{1,0:T(8,128)S(1)}, u32[]{:S(2)}, u32[]{:S(2)}) %collective-permute-start) | collective-permute-done | bytes 262176 | tf_op jit(solution)/shard_map/ppermute | solution.py:97
  108.8 6.5 %collective-permute-done.1 = f32[64,1024]{1,0:T(8,128)S(1)} collective-permute-done((f32[64,1024]{1,0:T(8,128)S(1)}, f32[64,1024]{1,0:T(8,128)S(1)}, u32[]{:S(2)}, u32[]{:S(2)}) %collective-permute-start.1) | collective-permute-done | bytes 262176 | tf_op jit(solution)/shard_map/ppermute | solution.py:97
  117.0 7.6 %collective-permute-done.2 = f32[64,1024]{1,0:T(8,128)S(1)} collective-permute-done((f32[64,1024]{1,0:T(8,128)S(1)}, f32[64,1024]{1,0:T(8,128)S(1)}, u32[]{:S(2)}, u32[]{:S(2)}) %collective-permute-start.2) | collective-permute-done | bytes 262176 | tf_op jit(solution)/shard_map/ppermute | solution.py:97
  127.7 6.8 %collective-permute-done.3 = f32[64,1024]{1,0:T(8,128)S(1)} collective-permute-done((f32[64,1024]{1,0:T(8,128)S(1)}, f32[64,1024]{1,0:T(8,128)S(1)}, u32[]{:S(2)}, u32[]{:S(2)}) %collective-permute-start.3) | collective-permute-done | bytes 262176 | tf_op jit(solution)/shard_map/ppermute | solution.py:97
  135.2 20.7 %psum.21 = f32[]{:T(128)} all-reduce(f32[]{:T(128)} %get-tuple-element.38), channel_id=1, replica_groups=mesh['rows'=16,'sub'=16] {'sub'}, use_global_device_ids=true, to_apply=%region_2.3 | all-reduce | flops 1 | bytes 8 | tf_op jit(solution)/shard_map/psum | solution.py:100
  157.9 45.3 %all-gather.5.cloned.1.call-done = f32[1024,1024]{1,0:T(8,128)} async-done(((f32[64,1024]{1,0:T(8,128)}), f32[1024,1024]{1,0:T(8,128)}) %all-gather.5.cloned.1.call-update) | async-done | bytes 4194320 | tf_op jit(solution)/shard_map/all_gather | solution.py:81
  203.2 6.5 %fusion.18 = f32[64,1024]{1,0:T(8,128)S(1)} fusion(f32[64,1024]{1,0:T(8,128)} %broadcast_divide_fusion, f32[1024,1024]{1,0:T(8,128)} %all-gather.5.cloned.1.call-done), kind=kOutput, calls=%fused_computation.30 | convolution fusion | flops 805306368 | bytes 4718592 | tf_op jit(solution)/shard_map/dot_general | solution.py:16
  212.4 4.2 convolution_multiply_fusion.2
  220.2 40.4 %all-gather.7.cloned.1.call-done = f32[1024,1024]{1,0:T(8,128)} async-done(((f32[64,1024]{1,0:T(8,128)}), f32[1024,1024]{1,0:T(8,128)}) %all-gather.7.cloned.1.call-update) | async-done | bytes 4194320 | tf_op jit(solution)/shard_map/all_gather | solution.py:81
  260.5 6.5 %fusion.20 = f32[64,1024]{1,0:T(8,128)S(1)} fusion(f32[64,1024]{1,0:T(8,128)} %multiply_add_fusion.1, f32[1024,1024]{1,0:T(8,128)} %all-gather.7.cloned.1.call-done), kind=kOutput, calls=%fused_computation.32 | convolution fusion | flops 805306368 | bytes 4718592 | tf_op jit(solution)/shard_map/dot_general | solution.py:16
  269.7 4.2 fusion.8
  277.5 40.3 %all-gather.9.cloned.1.call-done = f32[1024,1024]{1,0:T(8,128)} async-done(((f32[64,1024]{1,0:T(8,128)}), f32[1024,1024]{1,0:T(8,128)}) %all-gather.9.cloned.1.call-update) | async-done | bytes 4194320 | tf_op jit(solution)/shard_map/all_gather | solution.py:81
  317.8 6.5 %fusion.22 = f32[64,1024]{1,0:T(8,128)S(1)} fusion(f32[64,1024]{1,0:T(8,128)} %multiply_add_fusion, f32[1024,1024]{1,0:T(8,128)} %all-gather.9.cloned.1.call-done), kind=kOutput, calls=%fused_computation.34 | convolution fusion | flops 805306368 | bytes 4718592 | tf_op jit(solution)/shard_map/dot_general | solution.py:16
  327.0 4.2 fusion.7
  335.3 6.0 %all-to-all-start.1 = ((s32[16,4,256]{2,1,0:T(4,128)}), s32[16,4,256]{2,1,0:T(4,128)S(1)}, u32[]{:S(2)}, u32[]{:S(2)}) async-start(s32[16,4,256]{2,1,0:T(4,128)} %all_to_all.27), calls=%async_computation.1 | async-start | bytes 131072 | tf_op jit(solution)/shard_map/all_to_all | solution.py:113
  341.3 31.3 %all-gather.11.cloned.1.call-done = bf16[1024,1024]{1,0:T(8,128)(2,1)} async-done(((bf16[64,1024]{1,0:T(8,128)(2,1)}), bf16[1024,1024]{1,0:T(8,128)(2,1)}) %all-gather.11.cloned.1.call-update) | async-done | bytes 2097168 | tf_op jit(solution)/shard_map/all_gather | solution.py:108
  375.7 6.4 %all-to-all-start = ((bf16[256,16,64]{0,2,1:T(8,128)(2,1)}), bf16[256,16,64]{0,2,1:T(8,128)(2,1)S(1)}, u32[]{:S(2)}, u32[]{:S(2)}) async-start(bf16[256,16,64]{0,2,1:T(8,128)(2,1)} %bitcast.5), calls=%async_computation | async-start | bytes 1048576 | tf_op jit(solution)/shard_map/all_to_all | solution.py:112
  382.2 6.9 %fusion.3 = bf16[4,256]{1,0:T(4,128)(2,1)S(1)} fusion(s32[4,4096]{1,0:T(4,128)S(1)} %bitcast.54), kind=kLoop, calls=%fused_computation.5 | loop fusion | flops 12581888 | bytes 67584 | tf_op jit(solution)/shard_map/while/body/eval_jaxpr/reduce_sum | solution.py:58
  391.1 5.9 %all-to-all-done = bf16[256,16,64]{0,2,1:T(8,128)(2,1)S(1)} async-done(((bf16[256,16,64]{0,2,1:T(8,128)(2,1)}), bf16[256,16,64]{0,2,1:T(8,128)(2,1)S(1)}, u32[]{:S(2)}, u32[]{:S(2)}) %all-to-all-start) | async-done | bytes 524320 | tf_op jit(solution)/shard_map/all_to_all | solution.py:112
  400.8 74.2 %all-reduce = (bf16[256,64]{0,1:T(8,128)(2,1)S(1)}, bf16[256,4]{0,1:T(4,128)(2,1)S(1)}) all-reduce(bf16[256,64]{0,1:T(8,128)(2,1)S(1)} %bitcast.56, bf16[256,4]{0,1:T(4,128)(2,1)S(1)} %bitcast.57), channel_id=1, replica_groups=mesh['rows'=16,'sub'=16] {'rows'}, use_global_device_ids=true, to_apply=%region_3.4 | all-reduce | flops 17408 | bytes 69632 | tf_op jit(solution)/shard_map/psum | solution.py:116
  (53 shorter events, 44.1 us)
Async XLA Ops:
  7.2 24.1 %copy-start = (bf16[256,1024]{1,0:T(8,128)(2,1)S(1)}, bf16[256,1024]{1,0:T(8,128)(2,1)}, u32[]{:S(2)}) copy-start(bf16[256,1024]{1,0:T(8,128)(2,1)} %param.3) | copy-start | bytes 1572868
  7.2 90.4 %reduce-scatter.4.cloned.1.call-start = ((), (), s32[]{:S(2)}) async-start(), calls=%async_computation.7 | async-start | bytes 4456448 | tf_op jit(solution)/shard_map/reduce_scatter | solution.py:87
  39.4 163.9 %all-gather.5.cloned.1.call-start = ((), (), s32[]{:S(2)}) async-start(), calls=%async_computation.3 | async-start | bytes 4456448 | tf_op jit(solution)/shard_map/all_gather | solution.py:81
  97.6 7.1 %collective-permute-start = (f32[64,1024]{1,0:T(8,128)}, f32[64,1024]{1,0:T(8,128)S(1)}, u32[]{:S(2)}, u32[]{:S(2)}) collective-permute-start(f32[64,1024]{1,0:T(8,128)} %reduce-scatter.4.cloned.1.call-done), channel_id=1, source_target_pairs={{0,16},{16,0},{32,48},{48,32},{64,80},{80,64},{96,112},{112,96},{1... | collective-permute-start | bytes 786440 | tf_op jit(solution)/shard_map/ppermute | solution.py:97
  105.6 9.6 %collective-permute-start.1 = (f32[64,1024]{1,0:T(8,128)S(1)}, f32[64,1024]{1,0:T(8,128)S(1)}, u32[]{:S(2)}, u32[]{:S(2)}) collective-permute-start(f32[64,1024]{1,0:T(8,128)S(1)} %add.62), channel_id=1, source_target_pairs={{0,32},{16,48},{32,0},{48,16},{64,96},{80,112},{96,64},{112,80},{1... | collective-permute-start | bytes 786440 | tf_op jit(solution)/shard_map/ppermute | solution.py:97
  115.3 9.3 %collective-permute-start.2 = (f32[64,1024]{1,0:T(8,128)S(1)}, f32[64,1024]{1,0:T(8,128)S(1)}, u32[]{:S(2)}, u32[]{:S(2)}) collective-permute-start(f32[64,1024]{1,0:T(8,128)S(1)} %add.63), channel_id=1, source_target_pairs={{0,64},{16,80},{32,96},{48,112},{64,0},{80,16},{96,32},{112,48},{1... | collective-permute-start | bytes 786440 | tf_op jit(solution)/shard_map/ppermute | solution.py:97
  124.6 9.9 %collective-permute-start.3 = (f32[64,1024]{1,0:T(8,128)S(1)}, f32[64,1024]{1,0:T(8,128)S(1)}, u32[]{:S(2)}, u32[]{:S(2)}) collective-permute-start(f32[64,1024]{1,0:T(8,128)S(1)} %add.64), channel_id=1, source_target_pairs={{0,128},{16,144},{32,160},{48,176},{64,192},{80,208},{96,224},{112... | collective-permute-start | bytes 786440 | tf_op jit(solution)/shard_map/ppermute | solution.py:97
  157.4 103.2 %all-gather.7.cloned.1.call-start = ((), (), s32[]{:S(2)}) async-start(), calls=%async_computation.4 | async-start | bytes 4456448 | tf_op jit(solution)/shard_map/all_gather | solution.py:81
  203.2 6.5 %copy-start.1 = (f32[1024,1024]{1,0:T(8,128)S(1)}, f32[1024,1024]{1,0:T(8,128)}, u32[]{:S(2)}) copy-start(f32[1024,1024]{1,0:T(8,128)} %all-gather.5.cloned.1.call-done) | copy-start | bytes 12582916
  209.7 6.8 %copy-start.6 = (f32[64,1024]{1,0:T(8,128)S(1)}, f32[64,1024]{1,0:T(8,128)}, u32[]{:S(2)}) copy-start(f32[64,1024]{1,0:T(8,128)} %broadcast_divide_fusion) | copy-start | bytes 786436
  219.9 97.9 %all-gather.9.cloned.1.call-start = ((), (), s32[]{:S(2)}) async-start(), calls=%async_computation.5 | async-start | bytes 4456448 | tf_op jit(solution)/shard_map/all_gather | solution.py:81
  260.5 6.5 %copy-start.3 = (f32[1024,1024]{1,0:T(8,128)S(1)}, f32[1024,1024]{1,0:T(8,128)}, u32[]{:S(2)}) copy-start(f32[1024,1024]{1,0:T(8,128)} %all-gather.7.cloned.1.call-done) | copy-start | bytes 12582916
  267.0 6.8 %copy-start.5 = (f32[64,1024]{1,0:T(8,128)S(1)}, f32[64,1024]{1,0:T(8,128)}, u32[]{:S(2)}) copy-start(f32[64,1024]{1,0:T(8,128)} %multiply_add_fusion.1) | copy-start | bytes 786436
  277.2 95.4 %all-gather.11.cloned.1.call-start = ((), (), s32[]{:S(2)}) async-start(), calls=%async_computation.6 | async-start | bytes 2228224 | tf_op jit(solution)/shard_map/all_gather | solution.py:108
  317.8 6.5 %copy-start.2 = (f32[1024,1024]{1,0:T(8,128)S(1)}, f32[1024,1024]{1,0:T(8,128)}, u32[]{:S(2)}) copy-start(f32[1024,1024]{1,0:T(8,128)} %all-gather.9.cloned.1.call-done) | copy-start | bytes 12582916
  324.3 6.9 %copy-start.4 = (f32[64,1024]{1,0:T(8,128)S(1)}, f32[64,1024]{1,0:T(8,128)}, u32[]{:S(2)}) copy-start(f32[64,1024]{1,0:T(8,128)} %multiply_add_fusion) | copy-start | bytes 786436
  327.0 7.6 %copy-start.8 = (s32[64,256]{1,0:T(8,128)S(1)}, s32[64,256]{1,0:T(8,128)}, u32[]{:S(2)}) copy-start(s32[64,256]{1,0:T(8,128)} %param.4) | copy-start | bytes 196612
  335.3 40.5 %all-to-all-start.1 = ((s32[16,4,256]{2,1,0:T(4,128)}), s32[16,4,256]{2,1,0:T(4,128)S(1)}, u32[]{:S(2)}, u32[]{:S(2)}) async-start(s32[16,4,256]{2,1,0:T(4,128)} %all_to_all.27), calls=%async_computation.1 | async-start | bytes 131072 | tf_op jit(solution)/shard_map/all_to_all | solution.py:113
  375.7 21.3 %all-to-all-start = ((bf16[256,16,64]{0,2,1:T(8,128)(2,1)}), bf16[256,16,64]{0,2,1:T(8,128)(2,1)S(1)}, u32[]{:S(2)}, u32[]{:S(2)}) async-start(bf16[256,16,64]{0,2,1:T(8,128)(2,1)} %bitcast.5), calls=%async_computation | async-start | bytes 1048576 | tf_op jit(solution)/shard_map/all_to_all | solution.py:112
  391.1 83.9 %copy-start.7 = (bf16[256,64]{0,1:T(8,128)(2,1)S(1)}, bf16[256,64]{0,1:T(8,128)(2,1)}, u32[]{:S(2)}) copy-start(bf16[256,64]{0,1:T(8,128)(2,1)} %param.5) | copy-start | bytes 98308
Sparse Core Ops, SparseCore 0:
  39.5 58.0 reduce-scatter.3
  157.5 45.7 all-gather.4
  220.1 40.4 all-gather.6
  277.4 40.4 all-gather.8
  334.7 37.8 all-gather.10
